TPU v7x, 256 devices: a whole 4x4x8 slice. The times are simulated.
256 devices in a mesh: prow: 16 (over z, core), pcol: 16 (over y, x).
Axes of the slice: x: 4, y: 4, z: 8, core: 2. Of those that a mesh axis runs over, the one named last changes fastest.
Arguments:
- kernel: float32 [3, 16, 256, 3, 16, 256], P(None, 'prow', None, None, 'pcol'), as said below
Outputs:
- factored: float32 [3, 16, 256, 3, 16, 256], P(None, 'prow', None, None, 'pcol')
Inputs may be any that keep to these rules, and one draw needn't show every extreme that they name: kernel is symmetric (entry (a, b) equals entry (b, a)); every diagonal entry is 1.1, every off-diagonal entry lies in (0, 1], and the matrix is positive definite with smallest eigenvalue at least 0.1.
All inputs are finite; a program needn't handle non-finite values.
Results may differ from a plain program's by a relative error of at most 0.0003.
Values sent between devices are 32-bit elements; how exact they have to be, the bound alone decides.
No kernel may reach another device: no remote copies, remote signals or barrier semaphores. Data moves between devices by JAX's collectives and lax.ppermute only.
A program may use at most 64 MiB of HBM per device.

v0:
```python
import jax
import jax.numpy as jnp
from jax import lax
from jax.sharding import PartitionSpec as P

HIGH = lax.Precision.HIGHEST


def chol_and_inverse(block, eye):
    lower = jnp.linalg.cholesky(block)
    inverse = jax.scipy.linalg.solve_triangular(lower, eye, lower=True)
    return (lower, inverse)


def on_device(kernel):
    prow = lax.axis_index("prow")
    pcol = lax.axis_index("pcol")
    rows = lax.axis_size("prow")
    cols = lax.axis_size("pcol")
    lbr, blk, lbc = (kernel.shape[0], kernel.shape[2], kernel.shape[3])
    work = kernel.reshape(lbr, blk, lbc, blk)
    eye = jnp.eye(blk, dtype=jnp.float32)
    zero = jnp.zeros((blk, blk), jnp.float32)
    corner_blk = work[0, :, 0, :]
    slots = jnp.stack(
        [
            jnp.where((prow == 0) & (pcol == 0), corner_blk, zero),
            jnp.where((prow == 1) & (pcol == 0), corner_blk, zero),
            jnp.where((prow == 1) & (pcol == 1), corner_blk, zero),
        ]
    )
    corner = lax.psum(slots, ("prow", "pcol"))
    own_col = work[:, :, 0, :]
    row_slots = jnp.stack([jnp.where(pcol == 0, own_col, 0.0), jnp.where(pcol == 1, own_col, 0.0)])
    row_panel = lax.psum(row_slots, "pcol")
    own_row = work[0]
    col_slots = jnp.stack([jnp.where(prow == 0, own_row, 0.0), jnp.where(prow == 1, own_row, 0.0)])
    col_panel = lax.psum(col_slots, "prow")
    l0, w0 = chol_and_inverse(corner[0], eye)
    p10 = jnp.dot(corner[1], w0.T, precision=HIGH)
    s11 = corner[2] - jnp.dot(p10, p10.T, precision=HIGH)
    l1, w1 = chol_and_inverse(s11, eye)
    r0 = jnp.einsum("aik,jk->aij", row_panel[0], w0, precision=HIGH)
    r1 = row_panel[1] - jnp.einsum("aik,jk->aij", r0, p10, precision=HIGH)
    r1 = jnp.einsum("aik,jk->aij", r1, w1, precision=HIGH)
    c0t = jnp.einsum("ik,kbj->bij", w0, col_panel[0], precision=HIGH)
    c1t = jnp.transpose(col_panel[1], (1, 0, 2)) - jnp.einsum(
        "ik,bkj->bij", p10, c0t, precision=HIGH
    )
    c1t = jnp.einsum("ik,bkj->bij", w1, c1t, precision=HIGH)
    left = jnp.concatenate([r0, r1], axis=2)
    right = jnp.concatenate([c0t, c1t], axis=1)
    trailing = work - jnp.einsum("aik,bkj->aibj", left, right, precision=HIGH)
    row_ids = jnp.arange(lbr, dtype=jnp.int32) * rows + prow
    col_ids = jnp.arange(lbc, dtype=jnp.int32) * cols + pcol
    ri = row_ids[:, None, None, None]
    cj = col_ids[None, None, :, None]
    rk = row_ids[:, None, None]
    col0 = jnp.where(rk == 0, l0[None], r0)[:, :, None, :]
    col1 = jnp.where(rk == 0, 0.0, jnp.where(rk == 1, l1[None], r1))[:, :, None, :]
    out = jnp.where(cj == 0, col0, jnp.where(cj == 1, col1, trailing))
    out = jnp.where((ri < 2) & (cj > ri), 0.0, out)
    return out.reshape(kernel.shape)


def solution(mesh):
    spec = P(None, "prow", None, None, "pcol", None)
    return jax.shard_map(on_device, mesh=mesh, in_specs=(spec,), out_specs=spec, check_vma=False)
```

profile of v0, /device:TPU:2, one launch (start us, length us, event | category | flops | bytes accessed | tf_op | source)
XLA Modules:
  0.0 512.3 jit_solution(17465115443136146933)
XLA Ops:
  6.5 5.5 %copy.2 = f32[3,1,256,3,1,256]{2,5,3,0,4,1:T(8,128)S(1)} copy(f32[3,1,256,3,1,256]{5,4,3,2,1,0:T(1,128)} %param.4) | data formatting | bytes 4718592 | tf_op args[0]
  12.1 0.9 pad_maximum_fusion.2
  13.1 1.1 slice-done
  14.3 1.3 pad_maximum_fusion.1
  15.8 1.2 pad_maximum_fusion
  17.7 252.8 %all-reduce.5.cloned.1.call-done = f32[3,256,256]{1,2,0:T(8,128)} async-done(((f32[3,256,256]{1,2,0:T(8,128)}), f32[3,256,256]{1,2,0:T(8,128)}) %all-reduce.5.cloned.1.call-update) | async-done | bytes 786448 | tf_op jit(solution)/shard_map/psum | solution.py:32
  270.6 1.0 slice_bitcast_fusion.9
  271.7 1.0 fusion.9
  272.7 11.7 %cholesky.130 = f32[128,128]{1,0:T(8,128)S(1)} custom-call(f32[128,128]{1,0:T(8,128)S(1)} %cholesky.194), custom_call_target="Cholesky" | custom-call | tf_op jit(solution)/shard_map/jit(cholesky)/cholesky | solution.py:10
  284.4 9.8 %custom-call.13 = f32[1,128,128]{1,2,0:T(8,128)S(1)} custom-call(f32[1,128,128]{2,1,0:T(8,128)S(1)} %get-tuple-element.59), custom_call_target="InvertDiagBlocksLowerTriangular" | custom-call | tf_op jit(solution)/shard_map/jit(cholesky)/cholesky | solution.py:10
  294.7 11.7 %cholesky.147 = f32[128,128]{1,0:T(8,128)S(1)} custom-call(f32[128,128]{1,0:T(8,128)S(1)} %convolution_subtract_fusion.5), custom_call_target="Cholesky" | custom-call | tf_op jit(solution)/shard_map/jit(cholesky)/cholesky | solution.py:10
  306.5 0.7 compare_reduce_fusion.2
  308.5 0.8 fusion.16
  309.4 3.9 while.4
  309.4 0.6 fusion.59
  310.0 1.3 bitcast_dynamic-update-slice_fusion.4
  311.3 0.6 fusion.59
  312.0 1.3 bitcast_dynamic-update-slice_fusion.4
  313.3 19.8 %custom-call.14 = f32[2,128,128]{1,2,0:T(8,128)S(1)} custom-call(f32[2,128,128]{2,1,0:T(8,128)S(1)} %get-tuple-element.21), custom_call_target="InvertDiagBlocksLowerTriangular" | custom-call | tf_op jit(solution)/shard_map/jit(_solve_triangular)/triangular_solve | solution.py:11
  334.1 0.6 copy-done.1
  334.7 1.5 fusion.8
  336.3 1.4 convolution_subtract_fusion.1
  337.9 0.7 copy-done.12
  338.6 11.7 %cholesky.164 = f32[128,128]{1,0:T(8,128)S(1)} custom-call(f32[128,128]{1,0:T(8,128)S(1)} %cholesky.197), custom_call_target="Cholesky" | custom-call | tf_op jit(solution)/shard_map/jit(cholesky)/cholesky | solution.py:10
  350.3 9.8 %custom-call.15 = f32[1,128,128]{1,2,0:T(8,128)S(1)} custom-call(f32[1,128,128]{2,1,0:T(8,128)S(1)} %get-tuple-element.55), custom_call_target="InvertDiagBlocksLowerTriangular" | custom-call | tf_op jit(solution)/shard_map/jit(cholesky)/cholesky | solution.py:10
  360.2 1.0 constant_dynamic-update-slice_fusion.1
  361.2 1.1 convolution_subtract_fusion.4
  362.3 11.7 %cholesky.181 = f32[128,128]{1,0:T(8,128)S(1)} custom-call(f32[128,128]{1,0:T(8,128)S(1)} %convolution_subtract_fusion.4), custom_call_target="Cholesky" | custom-call | tf_op jit(solution)/shard_map/jit(cholesky)/cholesky | solution.py:10
  374.1 0.6 compare_reduce_fusion
  374.7 0.7 compare_reduce_fusion.1
  376.7 1.7 fusion.15
  378.4 3.9 while.5
  378.7 0.6 fusion.60
  379.2 1.2 bitcast_dynamic-update-slice_fusion.5
  381.1 1.2 bitcast_dynamic-update-slice_fusion.5
  382.3 19.7 %custom-call.16 = f32[2,128,128]{1,2,0:T(8,128)S(1)} custom-call(f32[2,128,128]{2,1,0:T(8,128)S(1)} %get-tuple-element.22), custom_call_target="InvertDiagBlocksLowerTriangular" | custom-call | tf_op jit(solution)/shard_map/jit(_solve_triangular)/triangular_solve | solution.py:11
  402.0 1.8 copy.10
  403.9 1.8 copy.4
  406.3 1.8 fusion.24
  408.1 2.1 convolution_bitcast_fusion.2
  410.2 0.9 fusion.4
  411.2 1.7 convolution_bitcast_fusion
  412.9 75.2 %all-reduce.7.cloned.1.call-done = f32[2,3,256,256]{2,3,1,0:T(8,128)} async-done(((f32[2,3,256,256]{2,3,1,0:T(8,128)}), f32[2,3,256,256]{2,3,1,0:T(8,128)}) %all-reduce.7.cloned.1.call-update) | async-done | bytes 1572880 | tf_op jit(solution)/shard_map/psum | solution.py:35
  488.1 2.1 fusion.5
  490.3 0.9 convolution_subtract_fusion
  491.4 0.9 broadcast_select_fusion
  492.6 6.2 %select_bitcast_fusion = f32[3,1,256,3,1,256]{2,5,3,0,4,1:T(8,128)} fusion(f32[3,256,256]{1,2,0:T(8,128)S(1)} %get-tuple-element.66, f32[3,256,256]{1,2,0:T(8,128)S(1)} %fusion.5, f32[3,256,256]{2,1,0:T(8,128)S(1)} %copy-done, f32[3,256,256]{2,1,0:T(8,128)S(1)} %convolution_bitcast_fusion.2, f32[3,256,256]{1,2,0:T(8,128)S(1)} %get-tuple-element.61, ...), kind=kOutput, calls=%fused_computation.4 | convolution fusion | flops 3627024384 | bytes 9437199 | tf_op jit(solution)/shard_map/aik,bkj->aibj/dot_general | solution.py:53
  498.8 6.6 %copy.15 = f32[3,1,256,3,1,256]{5,4,3,2,1,0:T(1,128)} copy(f32[3,1,256,3,1,256]{2,5,3,0,4,1:T(8,128)} %select_bitcast_fusion) | data formatting | bytes 4718592 | tf_op jit(solution)/shard_map/reshape | solution.py:63
  (77 shorter events, 4.8 us)
Async XLA Ops:
  6.5 264.0 %all-reduce.5.cloned.1.call-start = ((), (), s32[]{:S(2)}) async-start(), calls=%async_computation | async-start | bytes 1572864 | tf_op jit(solution)/shard_map/psum | solution.py:32
  13.0 1.1 slice-start
  13.1 395.0 %all-reduce.9.cloned.1.call-start = ((), (), s32[]{:S(2)}) async-start(), calls=%async_computation.2 | async-start | bytes 3145728 | tf_op jit(solution)/shard_map/psum | solution.py:38
  15.6 472.5 %all-reduce.7.cloned.1.call-start = ((), (), s32[]{:S(2)}) async-start(), calls=%async_computation.1 | async-start | bytes 3145728 | tf_op jit(solution)/shard_map/psum | solution.py:35
  313.3 19.9 %copy-start.15 = (s32[2,2]{1,0:T(2,128)}, s32[2,2]{1,0:T(2,128)S(1)}, u32[]{:S(2)}) copy-start(s32[2,2]{1,0:T(2,128)S(1)} %get-tuple-element.177) | copy-start | bytes 52
  334.1 0.7 copy-start.1
  337.8 0.7 copy-start.12
  338.6 39.8 %copy-start.16 = (s32[2,2]{1,0:T(2,128)S(1)}, s32[2,2]{1,0:T(2,128)}, u32[]{:S(2)}) copy-start(s32[2,2]{1,0:T(2,128)} %copy-done.15) | copy-start | bytes 52
  374.1 2.6 copy-start.11
  402.0 3.7 copy-start.13
  406.0 2.1 copy-start.2
  408.1 2.1 copy-start.5
  410.2 0.9 copy-start.3
  410.2 1.0 copy-start.7
  488.1 2.1 copy-start.6
  490.3 0.9 copy-start.4
  490.3 1.0 copy-start.8
  490.3 1.1 copy-start.9
  490.3 1.1 copy-start.10
  490.3 1.1 copy-start.14
  491.4 1.1 copy-start
Sparse Core Ops, SparseCore 0:
  13.2 257.3 all-reduce.4
  273.0 113.0 all-reduce.8
  389.4 98.6 all-reduce.6
where the time goes:
time: 523 us; the launch traced here: 512 us
  waiting for transfers between devices  328 us (63%)
  other arithmetic  116 us (22%)
  local copies, waits for them, and re-layouts  27.6 us (5%)
  matrix products  23.7 us (5%)
  between operations  16.5 us (3%)
    psum x1, waiting for transfers between devices, on_device(): corner = lax.psum(slots, ('prow', 'pcol'))  253 us
    psum x1, waiting for transfers between devices, on_device(): row_panel = lax.psum(row_slots, 'pcol')  75.2 us
    another operation x13, other arithmetic, chol_and_inverse(): lower = jnp.linalg.cholesky(block)  68.7 us
    another operation x5, other arithmetic, chol_and_inverse(): inverse = jax.scipy.linalg.solve_triangular(lower, eye, lower=True)  42 us
  transfers between devices with their start and end apart: 3, of which 2 were waited for; matrix products, arithmetic and copies ran while one was open for 28% of the time, Pallas kernels for 0%

commit v1 on v0

--- a/solution.py
+++ b/solution.py
@@ -32,7 +32,7 @@
     corner = lax.psum(slots, ("prow", "pcol"))
     own_col = work[:, :, 0, :]
     row_slots = jnp.stack([jnp.where(pcol == 0, own_col, 0.0), jnp.where(pcol == 1, own_col, 0.0)])
-    row_panel = lax.psum(row_slots, "pcol")
+    row_panel = jnp.sum(lax.all_gather(row_slots, "pcol"), axis=0)
     own_row = work[0]
     col_slots = jnp.stack([jnp.where(prow == 0, own_row, 0.0), jnp.where(prow == 1, own_row, 0.0)])
     col_panel = lax.psum(col_slots, "prow")

time: 523 us -> 552 us (1.055)
  other arithmetic: 116 us -> 130 us
  local copies, waits for them, and re-layouts: 27.6 us -> 36.4 us
    psum x1, waiting for transfers between devices: 253 us -> 331 us  [on_device(): corner = lax.psum(slots, ('prow', 'pcol'))]
    psum x1 -> x0, waiting for transfers between devices: 75.2 us -> none  [on_device(): row_panel = lax.psum(row_slots, 'pcol')]
    reduce_sum x0 -> x1, other arithmetic: none -> 10.5 us  [on_device(): row_panel = jnp.sum(lax.all_gather(row_slots, 'pcol'), axis=0)]
  transfers between devices with their start and end apart: 3 -> 3, of which waited for: 2 -> 1; matrix products, arithmetic and copies ran while one was open for 28% -> 28% of each run, Pallas kernels for 0% -> 0%
where the time goes in v1:
time: 552 us; the launch traced here: 541 us
  waiting for transfers between devices  331 us (60%)
  other arithmetic  130 us (24%)
  local copies, waits for them, and re-layouts  36.4 us (7%)
  matrix products  25.9 us (5%)
  between operations  18.3 us (3%)
    psum x1, waiting for transfers between devices, on_device(): corner = lax.psum(slots, ('prow', 'pcol'))  331 us
    another operation x13, other arithmetic, chol_and_inverse(): lower = jnp.linalg.cholesky(block)  70.6 us
    another operation x5, other arithmetic, chol_and_inverse(): inverse = jax.scipy.linalg.solve_triangular(lower, eye, lower=True)  42.1 us
  transfers between devices with their start and end apart: 3, of which 1 were waited for; matrix products, arithmetic and copies ran while one was open for 28% of the time, Pallas kernels for 0%

profile of v1, /device:TPU:2, one launch (start us, length us, event | category | flops | bytes accessed | tf_op | source)
XLA Modules:
  0.0 541.1 jit_solution(14877009718348884626)
XLA Ops:
  7.4 5.5 %copy.14 = f32[3,1,256,3,1,256]{2,5,3,0,4,1:T(8,128)S(1)} copy(f32[3,1,256,3,1,256]{5,4,3,2,1,0:T(1,128)} %param.4) | data formatting | bytes 4718592 | tf_op args[0]
  12.9 0.9 pad_maximum_fusion.2
  13.9 1.1 slice-done
  15.1 1.3 pad_maximum_fusion.1
  16.7 1.2 pad_maximum_fusion
  18.0 3.1 copy.19
  21.8 330.7 %all-reduce.4.cloned.1.call-done = f32[3,256,256]{1,2,0:T(8,128)} async-done(((f32[3,256,256]{1,2,0:T(8,128)}), f32[3,256,256]{1,2,0:T(8,128)}) %all-reduce.4.cloned.1.call-update) | async-done | bytes 786448 | tf_op jit(solution)/shard_map/psum | solution.py:32
  352.5 1.0 slice_bitcast_fusion.8
  353.6 1.0 fusion.9
  354.6 11.7 %cholesky.130 = f32[128,128]{1,0:T(8,128)S(1)} custom-call(f32[128,128]{1,0:T(8,128)S(1)} %cholesky.194), custom_call_target="Cholesky" | custom-call | tf_op jit(solution)/shard_map/jit(cholesky)/cholesky | solution.py:10
  366.4 9.8 %custom-call.13 = f32[1,128,128]{1,2,0:T(8,128)S(1)} custom-call(f32[1,128,128]{2,1,0:T(8,128)S(1)} %get-tuple-element.59), custom_call_target="InvertDiagBlocksLowerTriangular" | custom-call | tf_op jit(solution)/shard_map/jit(cholesky)/cholesky | solution.py:10
  376.6 11.7 %cholesky.147 = f32[128,128]{1,0:T(8,128)S(1)} custom-call(f32[128,128]{1,0:T(8,128)S(1)} %convolution_subtract_fusion.5), custom_call_target="Cholesky" | custom-call | tf_op jit(solution)/shard_map/jit(cholesky)/cholesky | solution.py:10
  388.4 0.7 compare_reduce_fusion.2
  390.5 4.1 while.4
  391.2 1.4 bitcast_dynamic-update-slice_fusion.4
  393.3 1.4 bitcast_dynamic-update-slice_fusion.4
  395.3 19.8 %custom-call.14 = f32[2,128,128]{1,2,0:T(8,128)S(1)} custom-call(f32[2,128,128]{2,1,0:T(8,128)S(1)} %get-tuple-element.21), custom_call_target="InvertDiagBlocksLowerTriangular" | custom-call | tf_op jit(solution)/shard_map/jit(_solve_triangular)/triangular_solve | solution.py:11
  415.1 0.8 copy.16
  416.8 1.6 fusion.8
  418.4 1.4 convolution_subtract_fusion.1
  419.8 0.8 copy.23
  420.7 1.0 fusion.12
  422.4 11.7 %cholesky.164 = f32[128,128]{1,0:T(8,128)S(1)} custom-call(f32[128,128]{1,0:T(8,128)S(1)} %cholesky.197), custom_call_target="Cholesky" | custom-call | tf_op jit(solution)/shard_map/jit(cholesky)/cholesky | solution.py:10
  434.7 10.4 %custom-call.15 = f32[1,128,128]{1,2,0:T(8,128)} custom-call(f32[1,128,128]{2,1,0:T(8,128)S(1)} %get-tuple-element.55), custom_call_target="InvertDiagBlocksLowerTriangular" | custom-call | tf_op jit(solution)/shard_map/jit(cholesky)/cholesky | solution.py:10
  445.1 1.1 constant_dynamic-update-slice_fusion.1
  446.2 1.1 convolution_subtract_fusion.4
  447.3 11.7 %cholesky.181 = f32[128,128]{1,0:T(8,128)S(1)} custom-call(f32[128,128]{1,0:T(8,128)S(1)} %convolution_subtract_fusion.4), custom_call_target="Cholesky" | custom-call | tf_op jit(solution)/shard_map/jit(cholesky)/cholesky | solution.py:10
  459.0 1.4 compare_reduce_fusion.1
  462.5 1.9 fusion.15
  464.4 1.8 copy.24
  466.2 5.4 %while.5 = (s32[]{:T(128)}, f32[256,256]{1,0:T(8,128)S(1)}, s32[2,2]{1,0:T(2,128)}, f32[2,128,128]{2,1,0:T(8,128)S(1)}, s32[]{:T(128)}) while((s32[]{:T(128)}, f32[256,256]{1,0:T(8,128)S(1)}, s32[2,2]{1,0:T(2,128)}, f32[2,128,128]{2,1,0:T(8,128)S(1)}, s32[]{:T(128)}) %tuple.65), condition=%wide.while_cond.clone, body=%wide.while_body.clone.sunk | while | flops 2 | bytes 131189 | solution.py:11
  467.5 1.4 bitcast_dynamic-update-slice_fusion.5
  470.2 1.4 bitcast_dynamic-update-slice_fusion.5
  471.6 20.3 %custom-call.16 = f32[2,128,128]{1,2,0:T(8,128)} custom-call(f32[2,128,128]{2,1,0:T(8,128)S(1)} %get-tuple-element.22), custom_call_target="InvertDiagBlocksLowerTriangular" | custom-call | tf_op jit(solution)/shard_map/jit(_solve_triangular)/triangular_solve | solution.py:11
  491.9 1.1 fusion.19
  493.4 1.8 fusion.24
  495.2 2.1 convolution_bitcast_fusion.2
  497.3 0.9 copy-done
  498.2 0.9 fusion.4
  499.2 1.8 convolution_bitcast_fusion
  500.9 10.5 %reduce_sum.9 = f32[2,3,256,256]{3,2,1,0:T(8,128)} reduce(f32[16,2,3,256,256]{4,3,2,1,0:T(8,128)} %bitcast.153, f32[]{:T(128)} %constant.77.clone.1), dimensions={0}, to_apply=%region_5.7 | reduce | flops 5898240 | bytes 26738692 | tf_op jit(solution)/shard_map/reduce_sum | solution.py:35
  511.4 2.1 fusion.5
  513.5 0.9 slice.93
  514.4 2.3 copy.40
  516.8 2.1 convolution_subtract_fusion
  518.9 0.9 broadcast_select_fusion
  520.3 6.3 %select_bitcast_fusion = f32[3,1,256,3,1,256]{2,5,3,0,4,1:T(8,128)} fusion(f32[3,256,256]{1,2,0:T(8,128)S(1)} %get-tuple-element.66, f32[3,256,256]{1,2,0:T(8,128)S(1)} %fusion.5, f32[3,256,256]{2,1,0:T(8,128)S(1)} %copy-done.3, f32[3,256,256]{2,1,0:T(8,128)S(1)} %copy-done.1, f32[3,256,256]{1,2,0:T(8,128)S(1)} %get-tuple-element.61, ...), kind=kOutput, calls=%fused_computation.4 | convolution fusion | flops 3627024384 | bytes 9437199 | tf_op jit(solution)/shard_map/aik,bkj->aibj/dot_general | solution.py:53
  526.6 6.6 %copy.29 = f32[3,1,256,3,1,256]{5,4,3,2,1,0:T(1,128)} copy(f32[3,1,256,3,1,256]{2,5,3,0,4,1:T(8,128)} %select_bitcast_fusion) | data formatting | bytes 4718592 | tf_op jit(solution)/shard_map/reshape | solution.py:63
  (81 shorter events, 10.2 us)
Async XLA Ops:
  7.4 345.1 %all-reduce.4.cloned.1.call-start = ((), (), s32[]{:S(2)}) async-start(), calls=%async_computation | async-start | bytes 1572864 | tf_op jit(solution)/shard_map/psum | solution.py:32
  13.9 1.1 slice-start
  13.9 481.3 %all-reduce.6.cloned.1.call-start = ((), (), s32[]{:S(2)}) async-start(), calls=%async_computation.1 | async-start | bytes 3145728 | tf_op jit(solution)/shard_map/psum | solution.py:38
  16.5 484.4 %all-gather.3.cloned.1.call-start = ((), (), s32[]{:S(2)}) async-start(), calls=%async_computation.2 | async-start | bytes 26738688 | tf_op jit(solution)/shard_map/all_gather | solution.py:35
  394.7 0.6 copy-start.16
  416.8 78.3 %copy-start.4 = (f32[128,256]{1,0:T(8,128)}, f32[128,256]{1,0:T(8,128)S(1)}, u32[]{:S(2)}) copy-start(f32[128,256]{1,0:T(8,128)S(1)} %fusion.28) | copy-start | bytes 393220
  421.6 0.7 copy-start.14
  460.4 2.0 copy-start.13
  493.1 2.1 copy-start.5
  495.2 3.0 copy-start.8
  497.3 0.9 copy-start
  498.2 0.9 copy-start.6
  498.2 1.0 copy-start.9
  511.4 2.1 copy-start.2
  516.7 2.1 copy-start.7
  516.7 2.1 copy-start.10
  516.8 2.1 copy-start.11
  516.8 2.1 copy-start.12
  516.8 2.1 copy-start.15
  518.9 1.1 copy-start.1
  518.9 1.4 copy-start.3
Sparse Core Ops, SparseCore 0:
  14.0 338.4 all-reduce.3
  354.9 112.8 all-reduce.5
Sparse Core Ops, SparseCore 1:
  21.2 162.5 all-gather.2
